TPU v7x, 32 devices: a whole 2x2x4 slice. The times are simulated.
32 devices in a mesh: sec: 4 (over y, x), dev: 8 (over z, core).
Axes of the slice: x: 2, y: 2, z: 4, core: 2. Of those that a mesh axis runs over, the one named last changes fastest.
Arguments:
- strain_rows: bfloat16 [65536, 128], P(('sec', 'dev')), may hold values from -6 to 6
- bands: int32 [65536], P(('sec', 'dev')), may hold values from 0 to 15
- damaged: int32 [4096], P(('sec', 'dev')), may hold values from 0 to 2047
- owner: int32 [4096, 1], P(('sec', 'dev')), may hold values from 0 to 31; in each aligned block of 128 rows (0 to 127, 128 to 255, ...) at most 8 rows name the same one
- first_layers: bfloat16 [4096, 4096], P(('sec', 'dev')), may hold values from -0.5 to 0.5
- middle_weight: bfloat16 [4096, 4096], P(None, 'sec'), may hold values from -0.09375 to 0.09375
- out_weight: bfloat16 [4096, 128], P('sec'), may hold values from -0.09375 to 0.09375
- band_scale: float32 [16, 4096], replicated, may hold values from 0.5 to 2
- back_weight: bfloat16 [128, 128], replicated, may hold values from -0.5 to 0.5
Outputs:
- response: bfloat16 [4096, 128], P(('sec', 'dev'))
Inputs may be any that keep to these rules, and one draw needn't show every extreme that they name: Among the 128 rows of one macro device no owner is named more than 8 times, a bound that some block reaches. `damaged`: indices into the listing device's own 2048 points.
All inputs are finite; a program needn't handle non-finite values.
Results may differ from a plain program's by a relative error of at most 0.014.
Values may be sent and summed in bfloat16 or wider, within the bound.
No kernel may reach another device: no remote copies, remote signals or barrier semaphores. Data moves between devices by JAX's collectives and lax.ppermute only.
A program may use at most 128 MiB of HBM per device.

v0:
```python
import jax
import jax.numpy as jnp
from jax import lax
from jax.sharding import PartitionSpec as P

PASSES = 2


def band_rows(band_values, band_scale):
    levels = jnp.arange(band_scale.shape[0], dtype=jnp.float32)
    picks = (band_values.astype(jnp.float32)[:, None] == levels[None, :]).astype(jnp.float32)
    return jnp.dot(
        picks, band_scale, precision=lax.Precision.HIGHEST, preferred_element_type=jnp.float32
    )


def first_hidden(row_block, weight_block, band_block, band_scale):
    mixed = jnp.dot(row_block, weight_block, preferred_element_type=jnp.float32) * band_rows(
        band_block, band_scale
    )
    return jax.nn.silu(mixed).astype(jnp.bfloat16)


def surrogate_tail(hidden_block, middle_weight, out_weight):
    middle = jax.nn.silu(
        jnp.dot(hidden_block, middle_weight, preferred_element_type=jnp.float32)
    ).astype(jnp.bfloat16)
    return jnp.dot(middle, out_weight, preferred_element_type=jnp.float32)


def per_device(
    strain_rows,
    bands,
    damaged,
    owner,
    first_layers,
    middle_weight,
    out_weight,
    band_scale,
    back_weight,
):
    count_all = lax.axis_size(("sec", "dev"))
    list_rows = damaged.shape[0]
    slot_count = max(2, 2 * list_rows // count_all)
    recv_rows = count_all * slot_count
    feat_width = strain_rows.shape[1]
    features = jnp.take(strain_rows, damaged, axis=0)
    band_local = jnp.take(bands, damaged)
    target_owner = owner[:, 0]
    matches = (target_owner[:, None] == jnp.arange(count_all, dtype=jnp.int32)[None, :]).astype(
        jnp.int32
    )
    slot_rank = jnp.sum((jnp.cumsum(matches, axis=0) - 1) * matches, axis=1)
    target = target_owner * slot_count + slot_rank
    dispatch = (jnp.arange(recv_rows, dtype=jnp.int32)[:, None] == target[None, :]).astype(
        jnp.bfloat16
    )
    send_band = jnp.dot(
        dispatch, band_local.astype(jnp.bfloat16)[:, None], preferred_element_type=jnp.float32
    ).astype(jnp.bfloat16)
    result = None
    for segment_index in range(PASSES):
        send_rows = jnp.dot(dispatch, features, preferred_element_type=jnp.float32).astype(
            jnp.bfloat16
        )
        got_rows, got_band = (
            lax.all_to_all(
                send_rows.reshape(count_all, slot_count, feat_width),
                ("sec", "dev"),
                split_axis=0,
                concat_axis=0,
                tiled=True,
            ),
            lax.all_to_all(
                send_band.reshape(count_all, slot_count),
                ("sec", "dev"),
                split_axis=0,
                concat_axis=0,
                tiled=True,
            ),
        )
        got_rows = got_rows.reshape(recv_rows, feat_width)
        got_band = got_band.reshape(recv_rows)
        hidden = first_hidden(got_rows, first_layers, got_band, band_scale)
        every_hidden = lax.all_gather(hidden, "sec", axis=0, tiled=True)
        partial_value = lax.psum_scatter(
            surrogate_tail(every_hidden, middle_weight, out_weight),
            "sec",
            scatter_dimension=0,
            tiled=True,
        )
        response = partial_value.astype(jnp.bfloat16)
        returned = lax.all_to_all(
            response.reshape(count_all, slot_count, response.shape[1]),
            ("sec", "dev"),
            split_axis=0,
            concat_axis=0,
            tiled=True,
        )
        returned = returned.reshape(recv_rows, response.shape[1])
        result = lax.dot_general(
            dispatch, returned, (((0,), (0,)), ((), ())), preferred_element_type=jnp.float32
        ).astype(jnp.bfloat16)
        if segment_index + 1 < PASSES:
            features = (
                features.astype(jnp.float32)
                + jnp.dot(result, back_weight, preferred_element_type=jnp.float32)
            ).astype(jnp.bfloat16)
    return result


def solution(mesh):
    in_specs = (
        P(("sec", "dev"), None),
        P(("sec", "dev")),
        P(("sec", "dev")),
        P(("sec", "dev"), None),
        P(("sec", "dev"), None),
        P(None, "sec"),
        P("sec", None),
        P(),
        P(),
    )
    out_specs = P(("sec", "dev"), None)
    return jax.shard_map(
        per_device, mesh=mesh, in_specs=in_specs, out_specs=out_specs, check_vma=False
    )
```

profile of v0, /device:TPU:0, one launch (start us, length us, event | category | flops | bytes accessed | tf_op | source)
XLA Modules:
  0.0 342.8 jit_solution(10192566044894200866)
XLA Ops:
  6.5 0.0 copy-start
  6.5 0.7 compare_select_fusion
  7.3 0.7 fusion.19
  8.0 0.2 reduce_window_sum.11
  8.2 0.8 select_reduce_fusion
  9.0 0.7 multiply_add_fusion
  9.7 1.6 gather_fusion.1
  11.3 0.8 fusion.5
  12.1 0.7 all_to_all.25
  12.9 7.3 %all-to-all-start.1 = ((bf16[32,1,8]{2,1,0:T(2,128)(2,1)}), bf16[32,1,8]{2,1,0:T(2,128)(2,1)S(1)}, u32[]{:S(2)}, u32[]{:S(2)}) async-start(bf16[32,1,8]{2,1,0:T(2,128)(2,1)} %all_to_all.25), calls=%async_computation.1 | async-start | bytes 32768 | tf_op jit(solution)/shard_map/all_to_all | solution.py:74
  20.2 0.7 compare_and_fusion
  20.9 1.8 gather_fusion
  22.6 0.8 fusion.2
  23.5 3.8 %all-to-all-done.1 = bf16[32,1,8]{2,1,0:T(2,128)(2,1)S(1)} async-done(((bf16[32,1,8]{2,1,0:T(2,128)(2,1)}), bf16[32,1,8]{2,1,0:T(2,128)(2,1)S(1)}, u32[]{:S(2)}, u32[]{:S(2)}) %all-to-all-start.1) | async-done | bytes 544 | tf_op jit(solution)/shard_map/all_to_all | solution.py:74
  27.3 2.6 all-to-all-start
  29.8 0.0 all-gather.3.cloned.1.call-start
  29.9 0.1 convert_reduce_fusion
  30.0 0.1 reshape.65
  30.0 4.7 %fusion.6 = f32[256,4096]{1,0:T(8,128)} fusion(f32[16,4096]{1,0:T(8,128)} %param.16, f32[256]{0:T(256)S(1)} %reshape.65), kind=kOutput, calls=%fused_computation.21 | convolution fusion | flops 201330688 | bytes 4457472 | tf_op jit(solution)/shard_map/dot_general | solution.py:12
  34.8 0.0 copy-start.1
  34.8 2.5 all-to-all-done
  37.2 0.0 copy-done
  37.2 4.9 %multiply_convert_fusion.3 = bf16[256,4096]{1,0:T(8,128)(2,1)} fusion(f32[256,4096]{1,0:T(8,128)} %fusion.6, bf16[128,4096]{1,0:T(8,128)(2,1)S(1)} %copy-done, bf16[32,8,128]{2,1,0:T(8,128)(2,1)S(1)} %all-to-all-done), kind=kOutput, calls=%fused_computation.7 | convolution fusion | flops 274726912 | bytes 7405568 | tf_op jit(solution)/shard_map/dot_general | solution.py:18
  42.2 0.0 all-gather.3.cloned.1.call-update
  42.2 0.0 copy-start.2
  42.2 0.2 reduce-scatter.3.cloned.1.call-start
  42.4 86.2 %all-gather.3.cloned.1.call-done = bf16[1024,4096]{1,0:T(8,128)(2,1)} async-done(((bf16[256,4096]{1,0:T(8,128)(2,1)}), bf16[1024,4096]{1,0:T(8,128)(2,1)}) %all-gather.3.cloned.1.call-update) | async-done | bytes 8388624 | tf_op jit(solution)/shard_map/all_gather | solution.py:85
  128.7 0.0 copy-done.1
  128.7 16.1 %fusion = f32[1024,128]{1,0:T(8,128)} fusion(bf16[1024,128]{1,0:T(8,128)(2,1)S(1)} %copy-done.1, bf16[1024,4096]{1,0:T(8,128)(2,1)} %all-gather.3.cloned.1.call-done, bf16[4096,1024]{1,0:T(8,128)(2,1)} %param.14), kind=kOutput, calls=%fused_computation.8 | convolution fusion | flops 8863612928 | bytes 17563648 | tf_op jit(solution)/shard_map/dot_general | solution.py:28
  144.7 0.0 reduce-scatter.3.cloned.1.call-update
  144.8 0.0 all-gather.5.cloned.1.call-start
  144.8 25.2 %reduce-scatter.3.cloned.1.call-done = f32[256,128]{1,0:T(8,128)} async-done(((f32[1024,128]{1,0:T(8,128)}), f32[256,128]{1,0:T(8,128)}) %reduce-scatter.3.cloned.1.call-update) | async-done | bytes 131088 | tf_op jit(solution)/shard_map/reduce_scatter | solution.py:86
  170.0 0.9 convert_bitcast_fusion.1
  170.9 11.8 %all_to_all.31 = bf16[32,8,128]{2,1,0:T(8,128)(2,1)S(1)} all-to-all(bf16[32,8,128]{2,1,0:T(8,128)(2,1)S(1)} %convert_bitcast_fusion.1), channel_id=1, replica_groups=mesh['sec'=4,'dev'=8] {'sec','dev'}, dimensions={0} | all-to-all | bytes 131072 | tf_op jit(solution)/shard_map/all_to_all | solution.py:93
  182.7 0.0 copy-done.2
  182.7 0.3 fusion.4
  183.0 0.2 fusion.3
  183.2 9.1 %all_to_all.32 = bf16[32,8,128]{2,1,0:T(8,128)(2,1)S(1)} all-to-all(bf16[32,8,128]{2,1,0:T(8,128)(2,1)S(1)} %fusion.3), channel_id=1, replica_groups=mesh['sec'=4,'dev'=8] {'sec','dev'}, dimensions={0} | all-to-all | bytes 131072 | tf_op jit(solution)/shard_map/all_to_all | solution.py:67
  192.3 4.9 %multiply_convert_fusion.1 = bf16[256,4096]{1,0:T(8,128)(2,1)} fusion(f32[256,4096]{1,0:T(8,128)} %fusion.6, bf16[128,4096]{1,0:T(8,128)(2,1)S(1)} %copy-done, bf16[32,8,128]{2,1,0:T(8,128)(2,1)S(1)} %all_to_all.32), kind=kOutput, calls=%fused_computation.5 | convolution fusion | flops 274726912 | bytes 7405568 | tf_op jit(solution)/shard_map/dot_general | solution.py:18
  197.2 0.0 all-gather.5.cloned.1.call-update
  197.2 0.3 reduce-scatter.5.cloned.1.call-start
  197.5 83.9 %all-gather.5.cloned.1.call-done = bf16[1024,4096]{1,0:T(8,128)(2,1)} async-done(((bf16[256,4096]{1,0:T(8,128)(2,1)}), bf16[1024,4096]{1,0:T(8,128)(2,1)}) %all-gather.5.cloned.1.call-update) | async-done | bytes 8388624 | tf_op jit(solution)/shard_map/all_gather | solution.py:85
  281.4 16.1 %fusion.1 = f32[1024,128]{1,0:T(8,128)} fusion(bf16[1024,128]{1,0:T(8,128)(2,1)S(1)} %copy-done.1, bf16[1024,4096]{1,0:T(8,128)(2,1)} %all-gather.5.cloned.1.call-done, bf16[4096,1024]{1,0:T(8,128)(2,1)} %param.14), kind=kOutput, calls=%fused_computation.9 | convolution fusion | flops 8863612928 | bytes 17563648 | tf_op jit(solution)/shard_map/dot_general | solution.py:28
  297.5 0.0 reduce-scatter.5.cloned.1.call-update
  297.5 25.3 %reduce-scatter.5.cloned.1.call-done = f32[256,128]{1,0:T(8,128)} async-done(((f32[1024,128]{1,0:T(8,128)}), f32[256,128]{1,0:T(8,128)}) %reduce-scatter.5.cloned.1.call-update) | async-done | bytes 131088 | tf_op jit(solution)/shard_map/reduce_scatter | solution.py:86
  322.8 0.9 convert_bitcast_fusion
  323.7 11.8 %all_to_all.33 = bf16[32,8,128]{2,1,0:T(8,128)(2,1)S(1)} all-to-all(bf16[32,8,128]{2,1,0:T(8,128)(2,1)S(1)} %convert_bitcast_fusion), channel_id=1, replica_groups=mesh['sec'=4,'dev'=8] {'sec','dev'}, dimensions={0} | all-to-all | bytes 131072 | tf_op jit(solution)/shard_map/all_to_all | solution.py:93
  335.5 0.8 convolution_convert_fusion.2
  (2 shorter events, 0.0 us)
Async XLA Ops:
  6.5 30.7 %copy-start = (bf16[128,4096]{1,0:T(8,128)(2,1)S(1)}, bf16[128,4096]{1,0:T(8,128)(2,1)}, u32[]{:S(2)}) copy-start(bf16[128,4096]{1,0:T(8,128)(2,1)} %param.13) | copy-start | bytes 3145732
  12.9 14.4 %all-to-all-start.1 = ((bf16[32,1,8]{2,1,0:T(2,128)(2,1)}), bf16[32,1,8]{2,1,0:T(2,128)(2,1)S(1)}, u32[]{:S(2)}, u32[]{:S(2)}) async-start(bf16[32,1,8]{2,1,0:T(2,128)(2,1)} %all_to_all.25), calls=%async_computation.1 | async-start | bytes 32768 | tf_op jit(solution)/shard_map/all_to_all | solution.py:74
  27.3 9.9 %all-to-all-start = ((bf16[32,8,128]{2,1,0:T(8,128)(2,1)}), bf16[32,8,128]{2,1,0:T(8,128)(2,1)S(1)}, u32[]{:S(2)}, u32[]{:S(2)}) async-start(bf16[32,8,128]{2,1,0:T(8,128)(2,1)} %fusion.2), calls=%async_computation | async-start | bytes 131072 | tf_op jit(solution)/shard_map/all_to_all | solution.py:67
  29.8 98.8 %all-gather.3.cloned.1.call-start = ((), (), s32[]{:S(2)}) async-start(), calls=%async_computation.7 | async-start | bytes 10485760 | tf_op jit(solution)/shard_map/all_gather | solution.py:85
  34.8 93.9 %copy-start.1 = (bf16[1024,128]{1,0:T(8,128)(2,1)S(1)}, bf16[1024,128]{1,0:T(8,128)(2,1)}, u32[]{:S(2)}) copy-start(bf16[1024,128]{1,0:T(8,128)(2,1)} %param.15) | copy-start | bytes 786436
  42.2 140.5 %copy-start.2 = (bf16[128,128]{1,0:T(8,128)(2,1)S(1)}, bf16[128,128]{1,0:T(8,128)(2,1)}, u32[]{:S(2)}) copy-start(bf16[128,128]{1,0:T(8,128)(2,1)} %param.17) | copy-start | bytes 98308
  42.2 127.8 %reduce-scatter.3.cloned.1.call-start = ((), (), s32[]{:S(2)}) async-start(), calls=%async_computation.8 | async-start | bytes 655360 | tf_op jit(solution)/shard_map/reduce_scatter | solution.py:86
  144.8 136.6 %all-gather.5.cloned.1.call-start = ((), (), s32[]{:S(2)}) async-start(), calls=%async_computation.9 | async-start | bytes 10485760 | tf_op jit(solution)/shard_map/all_gather | solution.py:85
  197.2 125.5 %reduce-scatter.5.cloned.1.call-start = ((), (), s32[]{:S(2)}) async-start(), calls=%async_computation.10 | async-start | bytes 655360 | tf_op jit(solution)/shard_map/reduce_scatter | solution.py:86
Sparse Core Ops, SparseCore 0:
  42.3 86.2 all-gather.2
  144.9 25.0 reduce-scatter.2
  197.4 83.9 all-gather.4
  297.7 25.0 reduce-scatter.4
where the time goes:
time: 343 us
  waiting for transfers between devices  227 us (66%)
  matrix products  49.8 us (15%)
  blocking collectives  32.6 us (10%)
  between operations  13.2 us (4%)
  starting transfers between devices  10.4 us (3%)
  other arithmetic  5.7 us (2%)
  local copies, waits for them, and re-layouts  4.2 us (1%)
    all_gather x2, waiting for transfers between devices, per_device(): every_hidden = lax.all_gather(hidden, 'sec', axis=0, tiled=True)  170 us
    reduce_scatter x2, waiting for transfers between devices, per_device(): lax.psum_scatter(surrogate_tail(every_hidden, middle_weight, out_weight),...  50.5 us
    dot_general x2, matrix products, surrogate_tail(): return jnp.dot(middle, out_weight, preferred_element_type=jnp.float32)  32.2 us
    all_to_all x2, blocking collectives, per_device(): lax.all_to_all(response.reshape(count_all, slot_count, response.shape[1])...  23.6 us
    dot_general x2, matrix products, first_hidden(): jnp.dot(row_block, weight_block, preferred_element_type=jnp.float32)  9.87 us
    all_to_all x1, blocking collectives, per_device(): lax.all_to_all(send_rows.reshape(count_all, slot_count, feat_width), ('se...  9.08 us
    all_to_all x1, starting transfers between devices, per_device(): lax.all_to_all(send_band.reshape(count_all, slot_count), ('sec', 'dev'),...  7.33 us
  transfers between devices with their start and end apart: 6, of which 6 were waited for; matrix products, arithmetic and copies ran while one was open for 2% of the time, Pallas kernels for 0%

commit v1 on v0

--- a/solution.py
+++ b/solution.py
@@ -82,7 +82,34 @@
         got_rows = got_rows.reshape(recv_rows, feat_width)
         got_band = got_band.reshape(recv_rows)
         hidden = first_hidden(got_rows, first_layers, got_band, band_scale)
-        every_hidden = lax.all_gather(hidden, "sec", axis=0, tiled=True)
+
+        def begin_counts(point, which_dim):
+            after = lax.axis_size("sec")
+            carry_out = lax.axis_index("sec")
+            upper, outer, kept_arr = (after, carry_out, point.shape[which_dim])
+            series = [dev * upper if m == which_dim else dev for m, dev in enumerate(point.shape)]
+            local_out = jnp.zeros(series, point.dtype)
+            fresh = lax.dynamic_update_slice_in_dim(
+                local_out, point, outer * kept_arr, axis=which_dim
+            )
+            nth = 1
+            o_now = last = point
+            while nth < upper // 2 + 1:
+                o_now = lax.ppermute(
+                    o_now, "sec", perm=[(m, (m + 1) % upper) for m in range(upper)]
+                )
+                fresh = lax.dynamic_update_slice_in_dim(
+                    fresh, o_now, (outer - nth) % upper * kept_arr, axis=which_dim
+                )
+                if 2 * nth < upper:
+                    last = lax.ppermute(last, "sec", [(m, (m - 1) % upper) for m in range(upper)])
+                    fresh = lax.dynamic_update_slice_in_dim(
+                        fresh, last, (outer + nth) % upper * kept_arr, axis=which_dim
+                    )
+                nth += 1
+            return fresh
+
+        every_hidden = begin_counts(hidden, 0)
         partial_value = lax.psum_scatter(
             surrogate_tail(every_hidden, middle_weight, out_weight),
             "sec",

time: 343 us -> 454 us (1.32)
  waiting for transfers between devices: 227 us -> 315 us
  local copies, waits for them, and re-layouts: 4.2 us -> 24.9 us
  starting transfers between devices: 10.4 us -> 15.8 us
    ppermute x0 -> x6, waiting for transfers between devices: none -> 264 us  [the longest x4 178 us: begin_counts(): lax.ppermute(o_now, 'sec', perm=[(m, (m + 1) % upper) for m in range(uppe...]
    all_gather x2 -> x0, waiting for transfers between devices: 170 us -> none  [per_device(): every_hidden = lax.all_gather(hidden, 'sec', axis=0, tiled=True)]
    dynamic_update_slice x0 -> x6, local copies, waits for them, and re-layouts: none -> 12.1 us  [the longest x4 7.57 us: begin_counts(): lax.dynamic_update_slice_in_dim(fresh, o_now, (outer - nth) % upper * kep...]
    another operation x0 -> x2, local copies, waits for them, and re-layouts: none -> 8.56 us
    ppermute x0 -> x6, starting transfers between devices: none -> 5.86 us  [the longest x2 4.52 us: begin_counts(): lax.ppermute(last, 'sec', [(m, (m - 1) % upper) for m in range(upper)])]
    reduce_scatter x2, waiting for transfers between devices: 50.5 us -> 44.9 us  [per_device(): lax.psum_scatter(surrogate_tail(every_hidden, middle_weight, out_weight),...]
  transfers between devices with their start and end apart: 6 -> 10, of which waited for: 6 -> 10; matrix products, arithmetic and copies ran while one was open for 2% -> 3% of each run, Pallas kernels for 0% -> 0%
where the time goes in v1:
time: 454 us
  waiting for transfers between devices  315 us (69%)
  matrix products  46.1 us (10%)
  blocking collectives  32.6 us (7%)
  local copies, waits for them, and re-layouts  24.9 us (5%)
  starting transfers between devices  15.8 us (3%)
  between operations  13.5 us (3%)
  other arithmetic  5.7 us (1%)
    ppermute x4, waiting for transfers between devices, begin_counts(): lax.ppermute(o_now, 'sec', perm=[(m, (m + 1) % upper) for m in range(uppe...  178 us
    ppermute x2, waiting for transfers between devices, begin_counts(): lax.ppermute(last, 'sec', [(m, (m - 1) % upper) for m in range(upper)])  85.4 us
    reduce_scatter x2, waiting for transfers between devices, per_device(): lax.psum_scatter(surrogate_tail(every_hidden, middle_weight, out_weight),...  44.9 us
    dot_general x2, matrix products, surrogate_tail(): return jnp.dot(middle, out_weight, preferred_element_type=jnp.float32)  32.2 us
    all_to_all x2, blocking collectives, per_device(): lax.all_to_all(response.reshape(count_all, slot_count, response.shape[1])...  23.6 us
  transfers between devices with their start and end apart: 10, of which 10 were waited for; matrix products, arithmetic and copies ran while one was open for 3% of the time, Pallas kernels for 0%

profile of v1, /device:TPU:0, one launch (start us, length us, event | category | flops | bytes accessed | tf_op | source)
XLA Modules:
  0.0 453.6 jit_solution(16223514607654764197)
XLA Ops:
  6.5 0.7 compare_select_fusion
  7.3 0.7 fusion.19
  8.0 0.2 reduce_window_sum.11
  8.2 0.8 select_reduce_fusion
  9.0 0.7 multiply_add_fusion
  9.7 1.6 gather_fusion.1
  11.3 0.8 fusion.5
  12.1 0.7 all_to_all.25
  12.9 7.3 %all-to-all-start.1 = ((bf16[32,1,8]{2,1,0:T(2,128)(2,1)}), bf16[32,1,8]{2,1,0:T(2,128)(2,1)S(1)}, u32[]{:S(2)}, u32[]{:S(2)}) async-start(bf16[32,1,8]{2,1,0:T(2,128)(2,1)} %all_to_all.25), calls=%async_computation.1 | async-start | bytes 32768 | tf_op jit(solution)/shard_map/all_to_all | solution.py:74
  20.2 0.7 compare_and_fusion
  20.9 1.8 gather_fusion
  22.6 0.9 fusion.2
  23.5 3.8 all-to-all-done.1
  27.3 2.6 all-to-all-start
  30.1 4.7 %fusion.6 = f32[256,4096]{1,0:T(8,128)} fusion(f32[16,4096]{1,0:T(8,128)} %param.16, f32[256]{0:T(256)S(1)} %reshape.65), kind=kOutput, calls=%fused_computation.21 | convolution fusion | flops 201330688 | bytes 4457472 | tf_op jit(solution)/shard_map/dot_general | solution.py:12
  34.8 2.4 all-to-all-done
  37.3 4.3 broadcast.29.clone
  41.5 3.4 constant_dynamic-update-slice_fusion.6
  45.0 0.7 collective-permute-start
  45.7 2.2 collective-permute-start.1
  47.9 46.7 %collective-permute-done = bf16[256,4096]{1,0:T(8,128)(2,1)S(1)} collective-permute-done((bf16[256,4096]{1,0:T(8,128)(2,1)}, bf16[256,4096]{1,0:T(8,128)(2,1)S(1)}, u32[]{:S(2)}, u32[]{:S(2)}) %collective-permute-start) | collective-permute-done | bytes 2097184 | tf_op jit(solution)/shard_map/ppermute | solution.py:98
  94.6 1.5 constant_dynamic-update-slice_fusion.5
  96.1 42.8 %collective-permute-done.1 = bf16[256,4096]{1,0:T(8,128)(2,1)} collective-permute-done((bf16[256,4096]{1,0:T(8,128)(2,1)}, bf16[256,4096]{1,0:T(8,128)(2,1)}, u32[]{:S(2)}, u32[]{:S(2)}) %collective-permute-start.1) | collective-permute-done | bytes 2097184 | tf_op jit(solution)/shard_map/ppermute | solution.py:105
  138.9 3.1 constant_dynamic-update-slice_fusion.4
  142.0 41.7 %collective-permute-done.2 = bf16[256,4096]{1,0:T(8,128)(2,1)} collective-permute-done((bf16[256,4096]{1,0:T(8,128)(2,1)S(1)}, bf16[256,4096]{1,0:T(8,128)(2,1)}, u32[]{:S(2)}, u32[]{:S(2)}) %collective-permute-start.2) | collective-permute-done | bytes 2097184 | tf_op jit(solution)/shard_map/ppermute | solution.py:98
  183.7 3.1 constant_dynamic-update-slice_fusion.3
  186.8 16.1 %fusion = f32[1024,128]{1,0:T(8,128)} fusion(bf16[1024,128]{1,0:T(8,128)(2,1)S(1)} %copy-done.3, bf16[1024,4096]{1,0:T(8,128)(2,1)} %constant_dynamic-update-slice_fusion.3, bf16[4096,1024]{1,0:T(8,128)(2,1)} %param.14), kind=kOutput, calls=%fused_computation.8 | convolution fusion | flops 8863612928 | bytes 17563648 | tf_op jit(solution)/shard_map/dot_general | solution.py:28
  203.0 23.1 %reduce-scatter.3.cloned.1.call-done = f32[256,128]{1,0:T(8,128)} async-done(((f32[1024,128]{1,0:T(8,128)}), f32[256,128]{1,0:T(8,128)}) %reduce-scatter.3.cloned.1.call-update) | async-done | bytes 131088 | tf_op jit(solution)/shard_map/reduce_scatter | solution.py:113
  226.1 0.9 convert_bitcast_fusion.1
  227.1 11.8 %all_to_all.31 = bf16[32,8,128]{2,1,0:T(8,128)(2,1)S(1)} all-to-all(bf16[32,8,128]{2,1,0:T(8,128)(2,1)S(1)} %convert_bitcast_fusion.1), channel_id=1, replica_groups=mesh['sec'=4,'dev'=8] {'sec','dev'}, dimensions={0} | all-to-all | bytes 131072 | tf_op jit(solution)/shard_map/all_to_all | solution.py:120
  238.8 0.3 fusion.4
  239.2 0.2 fusion.3
  239.3 9.1 %all_to_all.32 = bf16[32,8,128]{2,1,0:T(8,128)(2,1)S(1)} all-to-all(bf16[32,8,128]{2,1,0:T(8,128)(2,1)S(1)} %fusion.3), channel_id=1, replica_groups=mesh['sec'=4,'dev'=8] {'sec','dev'}, dimensions={0} | all-to-all | bytes 131072 | tf_op jit(solution)/shard_map/all_to_all | solution.py:67
  248.4 4.3 broadcast.29
  252.7 2.8 constant_dynamic-update-slice_fusion.2
  255.5 0.6 collective-permute-start.3
  256.1 2.3 collective-permute-start.4
  258.4 46.5 %collective-permute-done.3 = bf16[256,4096]{1,0:T(8,128)(2,1)S(1)} collective-permute-done((bf16[256,4096]{1,0:T(8,128)(2,1)S(1)}, bf16[256,4096]{1,0:T(8,128)(2,1)S(1)}, u32[]{:S(2)}, u32[]{:S(2)}) %collective-permute-start.3) | collective-permute-done | bytes 2097184 | tf_op jit(solution)/shard_map/ppermute | solution.py:98
  304.9 1.5 constant_dynamic-update-slice_fusion.1
  306.4 42.7 %collective-permute-done.4 = bf16[256,4096]{1,0:T(8,128)(2,1)S(1)} collective-permute-done((bf16[256,4096]{1,0:T(8,128)(2,1)S(1)}, bf16[256,4096]{1,0:T(8,128)(2,1)S(1)}, u32[]{:S(2)}, u32[]{:S(2)}) %collective-permute-start.4) | collective-permute-done | bytes 2097184 | tf_op jit(solution)/shard_map/ppermute | solution.py:105
  349.0 1.4 constant_dynamic-update-slice_fusion
  350.5 43.4 %collective-permute-done.5 = bf16[256,4096]{1,0:T(8,128)(2,1)S(1)} collective-permute-done((bf16[256,4096]{1,0:T(8,128)(2,1)S(1)}, bf16[256,4096]{1,0:T(8,128)(2,1)S(1)}, u32[]{:S(2)}, u32[]{:S(2)}) %collective-permute-start.5) | collective-permute-done | bytes 2097184 | tf_op jit(solution)/shard_map/ppermute | solution.py:98
  393.9 1.5 constant_dynamic-update-slice_fusion.7
  395.4 16.1 %fusion.1 = f32[1024,128]{1,0:T(8,128)} fusion(bf16[1024,128]{1,0:T(8,128)(2,1)S(1)} %copy-done.3, bf16[1024,4096]{1,0:T(8,128)(2,1)} %constant_dynamic-update-slice_fusion.7, bf16[4096,1024]{1,0:T(8,128)(2,1)} %param.14), kind=kOutput, calls=%fused_computation.9 | convolution fusion | flops 8863612928 | bytes 17563648 | tf_op jit(solution)/shard_map/dot_general | solution.py:28
  411.5 21.7 %reduce-scatter.5.cloned.1.call-done = f32[256,128]{1,0:T(8,128)} async-done(((f32[1024,128]{1,0:T(8,128)}), f32[256,128]{1,0:T(8,128)}) %reduce-scatter.5.cloned.1.call-update) | async-done | bytes 131088 | tf_op jit(solution)/shard_map/reduce_scatter | solution.py:113
  433.2 0.9 convert_bitcast_fusion
  434.1 11.8 %all_to_all.33 = bf16[32,8,128]{2,1,0:T(8,128)(2,1)S(1)} all-to-all(bf16[32,8,128]{2,1,0:T(8,128)(2,1)S(1)} %convert_bitcast_fusion), channel_id=1, replica_groups=mesh['sec'=4,'dev'=8] {'sec','dev'}, dimensions={0} | all-to-all | bytes 131072 | tf_op jit(solution)/shard_map/all_to_all | solution.py:120
  445.9 0.8 convolution_convert_fusion.2
  (20 shorter events, 0.3 us)
Async XLA Ops:
  6.5 35.0 %copy-start = (bf16[128,4096]{1,0:T(8,128)(2,1)S(1)}, bf16[128,4096]{1,0:T(8,128)(2,1)}, u32[]{:S(2)}) copy-start(bf16[128,4096]{1,0:T(8,128)(2,1)} %param.13) | copy-start | bytes 3145732
  12.9 14.4 %all-to-all-start.1 = ((bf16[32,1,8]{2,1,0:T(2,128)(2,1)}), bf16[32,1,8]{2,1,0:T(2,128)(2,1)S(1)}, u32[]{:S(2)}, u32[]{:S(2)}) async-start(bf16[32,1,8]{2,1,0:T(2,128)(2,1)} %all_to_all.25), calls=%async_computation.1 | async-start | bytes 32768 | tf_op jit(solution)/shard_map/all_to_all | solution.py:74
  27.3 10.0 %all-to-all-start = ((bf16[32,8,128]{2,1,0:T(8,128)(2,1)}), bf16[32,8,128]{2,1,0:T(8,128)(2,1)S(1)}, u32[]{:S(2)}, u32[]{:S(2)}) async-start(bf16[32,8,128]{2,1,0:T(8,128)(2,1)} %fusion.2), calls=%async_computation | async-start | bytes 131072 | tf_op jit(solution)/shard_map/all_to_all | solution.py:67
  29.9 196.3 %reduce-scatter.3.cloned.1.call-start = ((), (), s32[]{:S(2)}) async-start(), calls=%async_computation.7 | async-start | bytes 655360 | tf_op jit(solution)/shard_map/reduce_scatter | solution.py:113
  37.3 4.3 copy-start.1
  45.0 49.6 %collective-permute-start = (bf16[256,4096]{1,0:T(8,128)(2,1)}, bf16[256,4096]{1,0:T(8,128)(2,1)S(1)}, u32[]{:S(2)}, u32[]{:S(2)}) collective-permute-start(bf16[256,4096]{1,0:T(8,128)(2,1)} %get-tuple-element.6), channel_id=1, source_target_pairs={{0,8},{8,16},{16,24},{24,0},{1,9},{9,17},{17,25},{25,1},{2,10},{10... | collective-permute-start | bytes 6291464 | tf_op jit(solution)/shard_map/ppermute | solution.py:98
  45.7 93.2 %collective-permute-start.1 = (bf16[256,4096]{1,0:T(8,128)(2,1)}, bf16[256,4096]{1,0:T(8,128)(2,1)}, u32[]{:S(2)}, u32[]{:S(2)}) collective-permute-start(bf16[256,4096]{1,0:T(8,128)(2,1)} %get-tuple-element.6), channel_id=1, source_target_pairs={{0,24},{8,0},{16,8},{24,16},{1,25},{9,1},{17,9},{25,17},{2,26},{10... | collective-permute-start | bytes 6291464 | tf_op jit(solution)/shard_map/ppermute | solution.py:105
  94.6 89.1 %collective-permute-start.2 = (bf16[256,4096]{1,0:T(8,128)(2,1)S(1)}, bf16[256,4096]{1,0:T(8,128)(2,1)}, u32[]{:S(2)}, u32[]{:S(2)}) collective-permute-start(bf16[256,4096]{1,0:T(8,128)(2,1)S(1)} %collective-permute-done), channel_id=1, source_target_pairs={{0,8},{8,16},{16,24},{24,0},{1,9},{9,17},{17,25},{25,1},{2,10},{10... | collective-permute-start | bytes 6291464 | tf_op jit(solution)/shard_map/ppermute | solution.py:98
  96.1 90.8 %copy-start.3 = (bf16[1024,128]{1,0:T(8,128)(2,1)S(1)}, bf16[1024,128]{1,0:T(8,128)(2,1)}, u32[]{:S(2)}) copy-start(bf16[1024,128]{1,0:T(8,128)(2,1)} %param.15) | copy-start | bytes 786436
  186.8 52.0 %copy-start.4 = (bf16[128,128]{1,0:T(8,128)(2,1)S(1)}, bf16[128,128]{1,0:T(8,128)(2,1)}, u32[]{:S(2)}) copy-start(bf16[128,128]{1,0:T(8,128)(2,1)} %param.17) | copy-start | bytes 98308
  203.0 230.3 %reduce-scatter.5.cloned.1.call-start = ((), (), s32[]{:S(2)}) async-start(), calls=%async_computation.8 | async-start | bytes 655360 | tf_op jit(solution)/shard_map/reduce_scatter | solution.py:113
  248.4 4.3 copy-start.2
  255.5 49.4 %collective-permute-start.3 = (bf16[256,4096]{1,0:T(8,128)(2,1)S(1)}, bf16[256,4096]{1,0:T(8,128)(2,1)S(1)}, u32[]{:S(2)}, u32[]{:S(2)}) collective-permute-start(bf16[256,4096]{1,0:T(8,128)(2,1)S(1)} %get-tuple-element.8), channel_id=1, source_target_pairs={{0,8},{8,16},{16,24},{24,0},{1,9},{9,17},{17,25},{25,1},{2,10},{10... | collective-permute-start | bytes 6291464 | tf_op jit(solution)/shard_map/ppermute | solution.py:98
  256.1 92.9 %collective-permute-start.4 = (bf16[256,4096]{1,0:T(8,128)(2,1)S(1)}, bf16[256,4096]{1,0:T(8,128)(2,1)S(1)}, u32[]{:S(2)}, u32[]{:S(2)}) collective-permute-start(bf16[256,4096]{1,0:T(8,128)(2,1)S(1)} %get-tuple-element.8), channel_id=1, source_target_pairs={{0,24},{8,0},{16,8},{24,16},{1,25},{9,1},{17,9},{25,17},{2,26},{10... | collective-permute-start | bytes 6291464 | tf_op jit(solution)/shard_map/ppermute | solution.py:105
  304.9 89.0 %collective-permute-start.5 = (bf16[256,4096]{1,0:T(8,128)(2,1)S(1)}, bf16[256,4096]{1,0:T(8,128)(2,1)S(1)}, u32[]{:S(2)}, u32[]{:S(2)}) collective-permute-start(bf16[256,4096]{1,0:T(8,128)(2,1)S(1)} %collective-permute-done.3), channel_id=1, source_target_pairs={{0,8},{8,16},{16,24},{24,0},{1,9},{9,17},{17,25},{25,1},{2,10},{10... | collective-permute-start | bytes 6291464 | tf_op jit(solution)/shard_map/ppermute | solution.py:98
Sparse Core Ops, SparseCore 0:
  203.1 23.0 reduce-scatter.2
  411.6 21.5 reduce-scatter.4
